TPU v7x, 32 devices: a whole 2x2x4 slice. The times are simulated.
32 devices in a mesh: groups: 2 (over y), tp: 16 (over z, x, core).
Axes of the slice: x: 2, y: 2, z: 4, core: 2. Of those that a mesh axis runs over, the one named last changes fastest.
Arguments:
- hidden_in: bfloat16 [32, 8, 512], P(('groups', 'tp')), parts along dimension 0, may hold values from -6 to 6
- norm_gain: float32 [8192], replicated, may hold values from 0.1 to 1.9
- q_blocks: bfloat16 [16, 16, 128, 2048], P('tp'), may hold values from -0.0625 to 0.0625
- o_blocks: bfloat16 [16, 2048, 16, 128], P('tp'), may hold values from -1.5 to 1.5
- kv_blocks: bfloat16 [2, 1024, 8192], P(None, None, 'tp'), may hold values from -0.0625 to 0.0625
- kv_assign: int32 [16], replicated, may hold values from 0 to 7, as said below
- key_cache: bfloat16 [32, 8, 2048, 128], P(('groups', 'tp')), parts along dimension 0, may hold values from -240 to 240
- value_cache: bfloat16 [32, 8, 2048, 128], P(('groups', 'tp')), parts along dimension 0, may hold values from -6 to 6
- lengths: int32 [32, 8], P(('groups', 'tp')), parts along dimension 0, may hold values from 1 to 2048, as said below
Outputs:
- attn_out: bfloat16 [32, 8, 512], P(('groups', 'tp')), parts along dimension 0
There are 2 independent parts, one for each index of `groups`. A program takes and returns all parts, laid end to end along the dimension named above; an argument that names none is the same for every part. Nothing has to cross between parts.
Inputs may be any that keep to these rules, and one draw needn't show every extreme that they name: `kv_assign`: entries 2m and 2m + 1 are equal, and each of the 8 key-value heads is named by exactly two entries. `lengths`: in every rank one row has all 2048 positions valid.
All inputs are finite; a program needn't handle non-finite values.
Results may differ from a plain program's by a relative error of at most 0.011.
The roundings to bfloat16 on the way count: a program that leaves them out, or rounds other values in their place, can miss the bound.
Values may be sent and summed in bfloat16 or wider, within the bound.
No kernel may reach another device: no remote copies, remote signals or barrier semaphores. Data moves between devices by JAX's collectives and lax.ppermute only.
A program may use at most 128 MiB of HBM per device.

v0:
```python
import jax
import jax.numpy as jnp
from jax import lax
from jax.sharding import PartitionSpec as P

D = 8192
KVH = 8
HD = 128
ROLL = 16
ROWS = 8
GR = 4
QG = 16
DS = 512


def from_partner(value, axis, bit):
    mask = 2**bit
    pairs = [(source, source ^ mask) for source in range(lax.axis_size(axis))]
    return lax.ppermute(value, axis, pairs)


def norm_rows(rows_float, norm_gain):
    mean_square = jnp.mean(rows_float * rows_float, axis=-1, keepdims=True)
    return (rows_float * lax.rsqrt(mean_square + 1e-05) * norm_gain[None, :]).astype(jnp.bfloat16)


def local(
    hidden_in, norm_gain, q_blocks, o_blocks, kv_blocks, kv_assign, key_cache, value_cache, lengths
):
    ranks = lax.axis_size("tp")
    my_index = lax.axis_index("tp")
    my_rank = my_index % ROLL
    my_half = my_rank % 2
    grid_cols = ranks // GR
    group_count = ranks // ROLL
    col_width = q_blocks.shape[3]
    key_width = kv_blocks.shape[2]
    grid_row = my_index // grid_cols
    grid_col = my_index % grid_cols
    dest_ids = jnp.arange(ranks, dtype=jnp.int32)
    dest_rank = dest_ids % ROLL
    dest_head = kv_assign[dest_rank]
    dest_group = 2 * dest_head + dest_rank % 2
    dest_copy = dest_ids // ROLL
    every_rows = lax.all_gather(hidden_in, "tp", axis=0, tiled=True)
    rows_float = (
        every_rows.reshape(group_count, ROLL, ROWS, DS)
        .transpose(0, 2, 1, 3)
        .reshape(group_count * ROWS, D)
        .astype(jnp.float32)
    )
    normed_every = norm_rows(rows_float, norm_gain)
    col_rows = lax.dynamic_slice_in_dim(normed_every, grid_col * col_width, col_width, 1)
    query_part = jnp.einsum(
        "rc,aec->rae", col_rows, q_blocks[0], preferred_element_type=jnp.float32
    )
    query_part = (
        query_part.reshape(group_count, ROWS, QG, HD)
        .transpose(0, 2, 1, 3)
        .reshape(group_count * QG, ROWS, HD)
    )
    query_pick = jnp.take(query_part, dest_copy * QG + dest_group, axis=0)
    slot_mask = (jnp.arange(GR, dtype=jnp.int32) == grid_row).astype(jnp.float32)
    query_term = (query_pick[:, :, None, :] * slot_mask[None, None, :, None]).reshape(
        ranks, ROWS, GR * HD
    )
    key_rows = lax.dynamic_slice_in_dim(normed_every, my_index * key_width, key_width, 1)
    keyval_part = jnp.einsum("rc,kfc->rkf", key_rows, kv_blocks, preferred_element_type=jnp.float32)
    keyval_part = (
        keyval_part.reshape(group_count, ROWS, 2, KVH, HD)
        .transpose(0, 3, 1, 2, 4)
        .reshape(group_count * KVH, ROWS, 2 * HD)
    )
    keyval_term = jnp.take(keyval_part, dest_copy * KVH + dest_head, axis=0)
    proj_term = jnp.concatenate([query_term, keyval_term], -1).reshape(ranks * ROWS, (GR + 2) * HD)
    projected = lax.psum_scatter(proj_term, "tp", scatter_dimension=0, tiled=True)
    queries = projected[:, : GR * HD].astype(jnp.bfloat16)
    keyval_new = projected[:, GR * HD :].astype(jnp.bfloat16)
    key_new = keyval_new[:, :HD]
    value_new = keyval_new[:, HD:]
    partner_queries = from_partner(queries, "tp", 0)
    both_queries = jnp.where(
        my_half == 0,
        jnp.concatenate([queries, partner_queries], 1),
        jnp.concatenate([partner_queries, queries], 1),
    )
    both_queries = both_queries.reshape(ROWS, 2 * GR, HD)
    scale = 1.0 / HD**0.5
    scores = (
        jnp.einsum("bhe,bte->bht", both_queries, key_cache[0], preferred_element_type=jnp.float32)
        * scale
    )
    positions = jnp.arange(scores.shape[2], dtype=jnp.int32)
    masked = positions[None, None, :] < lengths[0][:, None, None]
    new_score = (
        jnp.einsum("bhe,be->bh", both_queries, key_new, preferred_element_type=jnp.float32) * scale
    )
    new_score = jnp.where(my_half == 0, new_score, jnp.float32(-1e30))
    top = jnp.maximum(jnp.max(jnp.where(masked, scores, jnp.float32(-1e30)), axis=-1), new_score)
    weights = jnp.where(masked, jnp.exp(scores - top[..., None]), jnp.float32(0.0))
    new_weight = jnp.exp(new_score - top)
    total = jnp.sum(weights, axis=-1) + new_weight
    summed = jnp.einsum(
        "bht,bte->bhe",
        weights.astype(jnp.bfloat16),
        value_cache[0],
        preferred_element_type=jnp.float32,
    )
    new_rounded = lax.optimization_barrier(new_weight.astype(jnp.bfloat16)).astype(jnp.float32)
    summed = summed + new_rounded[..., None] * value_new.astype(jnp.float32)[:, None, :]
    top_split = top.reshape(ROWS, 2, GR)
    total_split = total.reshape(ROWS, 2, GR)
    summed_split = summed.reshape(ROWS, 2, GR, HD)
    first_half = my_half == 0
    own_top = jnp.where(first_half, top_split[:, 0], top_split[:, 1])
    own_total = jnp.where(first_half, total_split[:, 0], total_split[:, 1])
    own_summed = jnp.where(first_half, summed_split[:, 0], summed_split[:, 1])
    give_top = jnp.where(first_half, top_split[:, 1], top_split[:, 0])
    give_total = jnp.where(first_half, total_split[:, 1], total_split[:, 0])
    give_summed = jnp.where(first_half, summed_split[:, 1], summed_split[:, 0])
    got_top, got_total, got_summed = from_partner((give_top, give_total, give_summed), "tp", 0)
    joint = jnp.maximum(own_top, got_top)
    factor_own = jnp.exp(own_top - joint)
    factor_got = jnp.exp(got_top - joint)
    numer = own_summed * factor_own[..., None] + got_summed * factor_got[..., None]
    denom = own_total * factor_own + got_total * factor_got
    attention = (numer / denom[..., None]).astype(jnp.bfloat16).reshape(ROWS, GR * HD)
    every_attn = lax.all_gather(attention[None], "tp", axis=0, tiled=True)
    head_ids = jnp.arange(KVH, dtype=jnp.int32)
    pair_heads = kv_assign[0::2]
    inverse = jnp.sum(
        head_ids[None, :] * (pair_heads[None, :] == head_ids[:, None]).astype(jnp.int32), axis=1
    )
    slot_ids = jnp.arange(QG, dtype=jnp.int32)
    rank_of_slot = 2 * inverse[slot_ids // 2] + slot_ids % 2
    attn_grid = every_attn.reshape(group_count, ROLL, ROWS, GR, HD)
    row_slot = lax.dynamic_index_in_dim(attn_grid, grid_row, 3, keepdims=False)
    chosen = jnp.take(row_slot, rank_of_slot, axis=1)
    out_part = jnp.einsum("gabe,cae->gbc", chosen, o_blocks[0], preferred_element_type=jnp.float32)
    placed = jnp.zeros((group_count, ROWS, D), jnp.float32)
    placed = lax.dynamic_update_slice_in_dim(placed, out_part, grid_col * col_width, 2)
    out_term = (
        placed.reshape(group_count, ROWS, ROLL, DS).transpose(0, 2, 1, 3).reshape(ranks * ROWS, DS)
    )
    my_cols = lax.psum_scatter(out_term, "tp", scatter_dimension=0, tiled=True)
    return my_cols.astype(jnp.bfloat16)[None]


def solution(mesh):
    return jax.shard_map(
        local,
        mesh=mesh,
        in_specs=(
            P(("groups", "tp"), None, None),
            P(),
            P("tp", None, None, None),
            P("tp", None, None, None),
            P(None, None, "tp"),
            P(),
            P(("groups", "tp"), None, None, None),
            P(("groups", "tp"), None, None, None),
            P(("groups", "tp"), None),
        ),
        out_specs=P(("groups", "tp"), None, None),
        check_vma=False,
    )
```

profile of v0, /device:TPU:0, one launch (start us, length us, event | category | flops | bytes accessed | tf_op | source)
XLA Modules:
  0.0 194.6 jit_solution(7086260716293882496)
XLA Ops:
  6.5 23.8 %all_gather.6 = bf16[16,8,512]{2,1,0:T(8,128)(2,1)S(1)} all-gather(bf16[1,8,512]{2,1,0:T(8,128)(2,1)} %param.9), channel_id=1, replica_groups=mesh['groups'=2,'tp'=16] {'tp'}, dimensions={0}, use_global_device_ids=true | all-gather | bytes 139264 | tf_op jit(solution)/shard_map/all_gather | solution.py:45
  30.3 0.2 multiply_reduce_fusion
  30.6 0.7 slice.41
  31.3 1.3 gather_fusion.1
  32.7 0.1 select_reduce_fusion.1
  32.8 0.7 gather_fusion
  33.6 0.9 multiply_convert_fusion
  34.4 0.6 convolution_bitcast_fusion
  35.1 0.1 broadcast_in_dim.83
  35.2 0.1 broadcast_in_dim.84
  35.3 5.6 %fusion.17 = f32[16,8,128]{2,1,0:T(8,128)S(1)} fusion(bf16[1,16,128,2048]{3,2,1,0:T(8,128)(2,1)} %param.11, bf16[8,8192]{1,0:T(8,128)(2,1)S(1)} %multiply_convert_fusion, s32[]{:T(128)S(6)} %select_n.308), kind=kOutput, calls=%fused_computation.16 | convolution fusion | flops 67108864 | bytes 8486916 | tf_op jit(solution)/shard_map/rc,aec->rae/dot_general | solution.py:54
  41.0 0.6 gather_fusion.2
  41.7 0.6 gather_fusion.3
  42.3 0.8 pad_maximum_fusion
  43.3 52.8 %reduce-scatter.3.cloned.1.call-done = f32[8,768]{1,0:T(8,128)} async-done(((f32[128,768]{1,0:T(8,128)}), f32[8,768]{1,0:T(8,128)}) %reduce-scatter.3.cloned.1.call-update) | async-done | bytes 24592 | tf_op jit(solution)/shard_map/reduce_scatter | solution.py:76
  96.1 0.7 convert.7
  96.9 1.2 collective-permute-done
  98.1 0.1 fusion.41
  98.2 3.5 %select_reduce_fusion = (f32[8,8]{1,0:T(8,128)S(1)}, f32[8,8,2048]{2,1,0:T(8,128)S(1)}) fusion(pred[8,2048]{1,0:T(8,128)(4,1)S(1)} %iota_compare_fusion, bf16[1,8,2048,128]{3,2,1,0:T(8,128)(2,1)} %param.15, bf16[8,4,128]{2,1,0:T(4,128)(2,1)S(1)} %concatenate.18, bf16[8,4,128]{2,1,0:T(4,128)(2,1)S(1)} %concatenate.17, pred[]{:T(512)S(6)} %eq.39), kind=kOutput, calls=%fused_computation.20 | convolution fusion | flops 34021312 | bytes 4751617 | tf_op jit(solution)/shard_map/bhe,bte->bht/dot_general | solution.py:90
  101.8 0.2 collective-permute-start.1
  101.9 0.3 fusion.23
  102.3 0.3 collective-permute-start.3
  102.6 2.9 %fusion.20 = f32[8,8,128]{2,1,0:T(8,128)S(1)} fusion(bf16[1,8,2048,128]{3,2,1,0:T(8,128)(2,1)} %param.16, f32[8,8,2048]{2,1,0:T(8,128)S(1)} %get-tuple-element.17, f32[8,8]{1,0:T(8,128)S(1)} %fusion.43, pred[8,2048]{1,0:T(8,128)(4,1)S(1)} %iota_compare_fusion, f32[8,128]{1,0:T(8,128)S(1)} %get-tuple-element.8, f32[8,8]{1,0:T(8,128)S(1)} %convert_element_type.57), kind=kOutput, calls=%fused_computation.18 | convolution fusion | flops 33964032 | bytes 4772352 | tf_op jit(solution)/shard_map/bht,bte->bhe/dot_general | solution.py:103
  105.6 0.2 collective-permute-start.2
  106.1 0.8 collective-permute-done.2
  106.8 0.1 fusion.38
  106.9 19.8 %all_gather.7 = bf16[16,8,512]{2,1,0:T(8,128)(2,1)S(1)} all-gather(bf16[1,8,512]{2,1,0:T(8,128)(2,1)S(1)} %broadcast_in_dim_reshape.3), channel_id=1, replica_groups=mesh['groups'=2,'tp'=16] {'tp'}, dimensions={0}, use_global_device_ids=true | all-gather | bytes 139264 | tf_op jit(solution)/shard_map/all_gather | solution.py:128
  126.7 0.6 gather_fusion.4
  127.3 5.7 %fusion.14 = f32[1,8,8192]{2,1,0:T(8,128)S(1)} fusion(f32[1,8,8192]{2,1,0:T(8,128)S(1)} %broadcast_in_dim.78, s32[]{:T(128)S(6)} %select_n.308, bf16[2048,16,128]{2,1,0:T(8,128)(2,1)} %bitcast.146, bf16[16,8,128]{2,1,0:T(8,128)(2,1)S(1)} %gather_fusion.4, pred[16]{0:T(512)(128)(4,1)S(1)} %get-tuple-element.18), kind=kOutput, calls=%fused_computation.15 | convolution fusion | flops 67125248 | bytes 8487428 | tf_op jit(solution)/shard_map/gabe,cae->gbc/dot_general | solution.py:139
  132.9 0.7 copy-done.1
  133.7 52.8 %reduce-scatter.5.cloned.1.call-done = f32[8,512]{1,0:T(8,128)} async-done(((f32[128,512]{1,0:T(8,128)}), f32[8,512]{1,0:T(8,128)}) %reduce-scatter.5.cloned.1.call-update) | async-done | bytes 16400 | tf_op jit(solution)/shard_map/reduce_scatter | solution.py:145
  186.4 1.3 convert_bitcast_fusion
  (49 shorter events, 1.1 us)
Async XLA Ops:
  6.5 27.9 %copy-start = (bf16[2,1024,512]{2,1,0:T(8,128)(2,1)S(1)}, bf16[2,1024,512]{2,1,0:T(8,128)(2,1)}, u32[]{:S(2)}) copy-start(bf16[2,1024,512]{2,1,0:T(8,128)(2,1)} %param.13) | copy-start | bytes 6291460
  6.5 89.6 %reduce-scatter.3.cloned.1.call-start = ((), (), s32[]{:S(2)}) async-start(), calls=%async_computation.2 | async-start | bytes 417792 | tf_op jit(solution)/shard_map/reduce_scatter | solution.py:76
  35.3 8.0 %copy-start.2 = (s32[1,8]{1,0:T(1,128)S(1)}, s32[1,8]{1,0:T(1,128)}, u32[]{:S(2)}) copy-start(s32[1,8]{1,0:T(1,128)} %param.17) | copy-start | bytes 100
  43.1 143.3 %reduce-scatter.5.cloned.1.call-start = ((), (), s32[]{:S(2)}) async-start(), calls=%async_computation.3 | async-start | bytes 278528 | tf_op jit(solution)/shard_map/reduce_scatter | solution.py:145
  96.9 1.2 collective-permute-start
  101.8 4.0 %collective-permute-start.1 = (f32[8,4]{0,1:T(4,128)S(1)}, f32[8,4]{0,1:T(4,128)S(1)}, u32[]{:S(2)}, u32[]{:S(2)}) collective-permute-start(f32[8,4]{0,1:T(4,128)S(1)} %select_bitcast_fusion.2), channel_id=1, source_target_pairs={{0,1},{1,0},{2,3},{3,2},{4,5},{5,4},{6,7},{7,6},{8,9},{9,8},{10,11... | collective-permute-start | bytes 392 | tf_op jit(solution)/shard_map/ppermute | solution.py:19
  102.3 3.5 %collective-permute-start.3 = (f32[8,4]{0,1:T(4,128)S(1)}, f32[8,4]{0,1:T(4,128)S(1)}, u32[]{:S(2)}, u32[]{:S(2)}) collective-permute-start(f32[8,4]{0,1:T(4,128)S(1)} %select_bitcast_fusion.1), channel_id=1, source_target_pairs={{0,1},{1,0},{2,3},{3,2},{4,5},{5,4},{6,7},{7,6},{8,9},{9,8},{10,11... | collective-permute-start | bytes 392 | tf_op jit(solution)/shard_map/ppermute | solution.py:19
  105.6 1.2 collective-permute-start.2
  132.9 0.7 copy-start.1
Sparse Core Ops, SparseCore 0:
  43.3 52.8 reduce-scatter.2
  133.8 52.5 reduce-scatter.4
where the time goes:
time: 195 us
  waiting for transfers between devices  107 us (55%)
  blocking collectives  43.5 us (22%)
  matrix products  18.4 us (9%)
  between operations  13.7 us (7%)
  local copies, waits for them, and re-layouts  5.86 us (3%)
  other arithmetic  4.78 us (2%)
    reduce_scatter x1, waiting for transfers between devices, local(): lax.psum_scatter(proj_term, 'tp', scatter_dimension=0, tiled=True)  52.8 us
    reduce_scatter x1, waiting for transfers between devices, local(): my_cols = lax.psum_scatter(out_term, 'tp', scatter_dimension=0, tiled=True)  52.8 us
    all_gather x1, blocking collectives, local(): every_rows = lax.all_gather(hidden_in, 'tp', axis=0, tiled=True)  23.8 us
    all_gather x1, blocking collectives, local(): every_attn = lax.all_gather(attention[None], 'tp', axis=0, tiled=True)  19.8 us
    dot_general x1, matrix products, local(): jnp.einsum('gabe,cae->gbc', chosen, o_blocks[0], preferred_element_type=j...  5.65 us
    dot_general x1, matrix products, local(): jnp.einsum('rc,aec->rae', col_rows, q_blocks[0], preferred_element_type=j...  5.65 us
  transfers between devices with their start and end apart: 6, of which 4 were waited for; matrix products, arithmetic and copies ran while one was open for 2% of the time, Pallas kernels for 0%

commit v1 on v0

--- a/solution.py
+++ b/solution.py
@@ -42,7 +42,21 @@
     dest_head = kv_assign[dest_rank]
     dest_group = 2 * dest_head + dest_rank % 2
     dest_copy = dest_ids // ROLL
-    every_rows = lax.all_gather(hidden_in, "tp", axis=0, tiled=True)
+    ways, here, turn = (lax.axis_size("tp"), lax.axis_index("tp"), hidden_in.shape[0])
+    dims = [n * ways if d == 0 else n for d, n in enumerate(hidden_in.shape)]
+    full = lax.dynamic_update_slice_in_dim(
+        jnp.zeros(dims, hidden_in.dtype), hidden_in, here * turn, axis=0
+    )
+    going_up = going_down = hidden_in
+    for far in range(1, ways // 2 + 1):
+        going_up = lax.ppermute(going_up, "tp", [(d, (d + 1) % ways) for d in range(ways)])
+        full = lax.dynamic_update_slice_in_dim(full, going_up, (here - far) % ways * turn, axis=0)
+        if 2 * far < ways:
+            going_down = lax.ppermute(going_down, "tp", [(d, (d - 1) % ways) for d in range(ways)])
+            full = lax.dynamic_update_slice_in_dim(
+                full, going_down, (here + far) % ways * turn, axis=0
+            )
+    every_rows = full
     rows_float = (
         every_rows.reshape(group_count, ROLL, ROWS, DS)
         .transpose(0, 2, 1, 3)

time: 195 us -> 218 us (1.12)
  starting transfers between devices: 0.8 us -> 32.8 us
  blocking collectives: 43.5 us -> 19.8 us
  waiting for transfers between devices: 107 us -> 122 us
    ppermute x0 -> x15, starting transfers between devices: none -> 32 us  [the longest x7 31.4 us: local(): lax.ppermute(going_down, 'tp', [(d, (d - 1) % ways) for d in range(ways)])]
    all_gather x1 -> x0, blocking collectives: 23.8 us -> none  [local(): every_rows = lax.all_gather(hidden_in, 'tp', axis=0, tiled=True)]
    ppermute x0 -> x15, waiting for transfers between devices: none -> 13.9 us  [the longest x8 13.7 us: local(): lax.ppermute(going_up, 'tp', [(d, (d + 1) % ways) for d in range(ways)])]
  transfers between devices with their start and end apart: 6 -> 21, of which waited for: 4 -> 11; matrix products, arithmetic and copies ran while one was open for 2% -> 3% of each run, Pallas kernels for 0% -> 0%
where the time goes in v1:
time: 218 us
  waiting for transfers between devices  122 us (56%)
  starting transfers between devices  32.8 us (15%)
  blocking collectives  19.8 us (9%)
  matrix products  18.4 us (8%)
  between operations  13.8 us (6%)
  local copies, waits for them, and re-layouts  6.6 us (3%)
  other arithmetic  4.79 us (2%)
    reduce_scatter x1, waiting for transfers between devices, local(): lax.psum_scatter(proj_term, 'tp', scatter_dimension=0, tiled=True)  53.3 us
    reduce_scatter x1, waiting for transfers between devices, local(): my_cols = lax.psum_scatter(out_term, 'tp', scatter_dimension=0, tiled=True)  52.7 us
    ppermute x7, starting transfers between devices, local(): lax.ppermute(going_down, 'tp', [(d, (d - 1) % ways) for d in range(ways)])  31.4 us
    all_gather x1, blocking collectives, local(): every_attn = lax.all_gather(attention[None], 'tp', axis=0, tiled=True)  19.8 us
    ppermute x8, waiting for transfers between devices, local(): lax.ppermute(going_up, 'tp', [(d, (d + 1) % ways) for d in range(ways)])  13.7 us
    dot_general x1, matrix products, local(): jnp.einsum('gabe,cae->gbc', chosen, o_blocks[0], preferred_element_type=j...  5.65 us
    dot_general x1, matrix products, local(): jnp.einsum('rc,aec->rae', col_rows, q_blocks[0], preferred_element_type=j...  5.65 us
  transfers between devices with their start and end apart: 21, of which 11 were waited for; matrix products, arithmetic and copies ran while one was open for 3% of the time, Pallas kernels for 0%

profile of v1, /device:TPU:0, one launch (start us, length us, event | category | flops | bytes accessed | tf_op | source)
XLA Modules:
  0.0 218.0 jit_solution(14329376513547302259)
XLA Ops:
  7.0 5.0 %collective-permute-start.1 = (bf16[1,8,512]{2,1,0:T(8,128)(2,1)}, bf16[1,8,512]{2,1,0:T(8,128)(2,1)S(1)}, u32[]{:S(2)}, u32[]{:S(2)}) collective-permute-start(bf16[1,8,512]{2,1,0:T(8,128)(2,1)} %param.9), channel_id=1, source_target_pairs={{0,15},{1,0},{2,1},{3,2},{4,3},{5,4},{6,5},{7,6},{8,7},{9,8},{10,9... | collective-permute-start | bytes 24584 | tf_op jit(solution)/shard_map/ppermute | solution.py:55
  12.0 0.7 slice.41
  12.7 1.3 gather_fusion.1
  14.2 0.7 gather_fusion
  15.0 0.7 bitcast_dynamic-update-slice_fusion.15
  16.1 4.4 %collective-permute-start.3 = (bf16[1,8,512]{2,1,0:T(8,128)(2,1)S(1)}, bf16[1,8,512]{2,1,0:T(8,128)(2,1)S(1)}, u32[]{:S(2)}, u32[]{:S(2)}) collective-permute-start(bf16[1,8,512]{2,1,0:T(8,128)(2,1)S(1)} %collective-permute-done.1), channel_id=1, source_target_pairs={{0,15},{1,0},{2,1},{3,2},{4,3},{5,4},{6,5},{7,6},{8,7},{9,8},{10,9... | collective-permute-start | bytes 24584 | tf_op jit(solution)/shard_map/ppermute | solution.py:55
  20.5 1.4 collective-permute-done.2
  21.9 4.4 %collective-permute-start.5 = (bf16[1,8,512]{2,1,0:T(8,128)(2,1)S(1)}, bf16[1,8,512]{2,1,0:T(8,128)(2,1)S(1)}, u32[]{:S(2)}, u32[]{:S(2)}) collective-permute-start(bf16[1,8,512]{2,1,0:T(8,128)(2,1)S(1)} %collective-permute-done.3), channel_id=1, source_target_pairs={{0,15},{1,0},{2,1},{3,2},{4,3},{5,4},{6,5},{7,6},{8,7},{9,8},{10,9... | collective-permute-start | bytes 24584 | tf_op jit(solution)/shard_map/ppermute | solution.py:55
  26.3 1.3 collective-permute-done.4
  27.7 4.4 %collective-permute-start.7 = (bf16[1,8,512]{2,1,0:T(8,128)(2,1)S(1)}, bf16[1,8,512]{2,1,0:T(8,128)(2,1)S(1)}, u32[]{:S(2)}, u32[]{:S(2)}) collective-permute-start(bf16[1,8,512]{2,1,0:T(8,128)(2,1)S(1)} %collective-permute-done.5), channel_id=1, source_target_pairs={{0,15},{1,0},{2,1},{3,2},{4,3},{5,4},{6,5},{7,6},{8,7},{9,8},{10,9... | collective-permute-start | bytes 24584 | tf_op jit(solution)/shard_map/ppermute | solution.py:55
  32.1 1.3 collective-permute-done.6
  33.4 4.4 %collective-permute-start.9 = (bf16[1,8,512]{2,1,0:T(8,128)(2,1)S(1)}, bf16[1,8,512]{2,1,0:T(8,128)(2,1)S(1)}, u32[]{:S(2)}, u32[]{:S(2)}) collective-permute-start(bf16[1,8,512]{2,1,0:T(8,128)(2,1)S(1)} %collective-permute-done.7), channel_id=1, source_target_pairs={{0,15},{1,0},{2,1},{3,2},{4,3},{5,4},{6,5},{7,6},{8,7},{9,8},{10,9... | collective-permute-start | bytes 24584 | tf_op jit(solution)/shard_map/ppermute | solution.py:55
  37.8 1.3 collective-permute-done.8
  39.2 4.4 %collective-permute-start.11 = (bf16[1,8,512]{2,1,0:T(8,128)(2,1)S(1)}, bf16[1,8,512]{2,1,0:T(8,128)(2,1)S(1)}, u32[]{:S(2)}, u32[]{:S(2)}) collective-permute-start(bf16[1,8,512]{2,1,0:T(8,128)(2,1)S(1)} %collective-permute-done.9), channel_id=1, source_target_pairs={{0,15},{1,0},{2,1},{3,2},{4,3},{5,4},{6,5},{7,6},{8,7},{9,8},{10,9... | collective-permute-start | bytes 24584 | tf_op jit(solution)/shard_map/ppermute | solution.py:55
  43.6 1.3 collective-permute-done.10
  45.0 4.4 %collective-permute-start.13 = (bf16[1,8,512]{2,1,0:T(8,128)(2,1)S(1)}, bf16[1,8,512]{2,1,0:T(8,128)(2,1)S(1)}, u32[]{:S(2)}, u32[]{:S(2)}) collective-permute-start(bf16[1,8,512]{2,1,0:T(8,128)(2,1)S(1)} %collective-permute-done.11), channel_id=1, source_target_pairs={{0,15},{1,0},{2,1},{3,2},{4,3},{5,4},{6,5},{7,6},{8,7},{9,8},{10,9... | collective-permute-start | bytes 24584 | tf_op jit(solution)/shard_map/ppermute | solution.py:55
  49.4 1.3 collective-permute-done.12
  50.8 5.7 %collective-permute-done.14 = bf16[1,8,512]{2,1,0:T(8,128)(2,1)S(1)} collective-permute-done((bf16[1,8,512]{2,1,0:T(8,128)(2,1)S(1)}, bf16[1,8,512]{2,1,0:T(8,128)(2,1)S(1)}, u32[]{:S(2)}, u32[]{:S(2)}) %collective-permute-start.14) | collective-permute-done | bytes 8224 | tf_op jit(solution)/shard_map/ppermute | solution.py:52
  56.7 0.9 multiply_convert_fusion
  58.3 5.7 %fusion.17 = f32[16,8,128]{2,1,0:T(8,128)S(1)} fusion(bf16[1,16,128,2048]{3,2,1,0:T(8,128)(2,1)} %param.11, bf16[8,8192]{1,0:T(8,128)(2,1)S(1)} %multiply_convert_fusion, s32[]{:T(128)S(6)} %select_n.447), kind=kOutput, calls=%fused_computation.16 | convolution fusion | flops 67108864 | bytes 8486916 | tf_op jit(solution)/shard_map/rc,aec->rae/dot_general | solution.py:68
  65.3 0.8 pad_maximum_fusion
  66.3 53.3 %reduce-scatter.3.cloned.1.call-done = f32[8,768]{1,0:T(8,128)} async-done(((f32[128,768]{1,0:T(8,128)}), f32[8,768]{1,0:T(8,128)}) %reduce-scatter.3.cloned.1.call-update) | async-done | bytes 24592 | tf_op jit(solution)/shard_map/reduce_scatter | solution.py:90
  119.6 0.7 convert.6
  120.3 1.2 collective-permute-done.15
  121.6 3.5 %select_reduce_fusion = (f32[8,8]{1,0:T(8,128)S(1)}, f32[8,8,2048]{2,1,0:T(8,128)S(1)}) fusion(pred[8,2048]{1,0:T(8,128)(4,1)S(1)} %iota_compare_fusion, bf16[1,8,2048,128]{3,2,1,0:T(8,128)(2,1)} %param.15, bf16[8,4,128]{2,1,0:T(4,128)(2,1)S(1)} %concatenate.18, bf16[8,4,128]{2,1,0:T(4,128)(2,1)S(1)} %concatenate.17, pred[]{:T(512)S(6)} %eq.54), kind=kOutput, calls=%fused_computation.20 | convolution fusion | flops 34021312 | bytes 4751617 | tf_op jit(solution)/shard_map/bhe,bte->bht/dot_general | solution.py:104
  126.1 2.9 %fusion.20 = f32[8,8,128]{2,1,0:T(8,128)S(1)} fusion(bf16[1,8,2048,128]{3,2,1,0:T(8,128)(2,1)} %param.16, f32[8,8,2048]{2,1,0:T(8,128)S(1)} %get-tuple-element.17, f32[8,8]{1,0:T(8,128)S(1)} %fusion.45, pred[8,2048]{1,0:T(8,128)(4,1)S(1)} %iota_compare_fusion, f32[8,128]{1,0:T(8,128)S(1)} %get-tuple-element.8, f32[8,8]{1,0:T(8,128)S(1)} %convert_element_type.52), kind=kOutput, calls=%fused_computation.18 | convolution fusion | flops 33964032 | bytes 4772352 | tf_op jit(solution)/shard_map/bht,bte->bhe/dot_general | solution.py:117
  129.5 0.8 collective-permute-done.17
  130.3 19.8 %all_gather.3 = bf16[16,8,512]{2,1,0:T(8,128)(2,1)S(1)} all-gather(bf16[1,8,512]{2,1,0:T(8,128)(2,1)S(1)} %broadcast_in_dim_reshape.3), channel_id=1, replica_groups=mesh['groups'=2,'tp'=16] {'tp'}, dimensions={0}, use_global_device_ids=true | all-gather | bytes 139264 | tf_op jit(solution)/shard_map/all_gather | solution.py:142
  150.7 5.7 %fusion.14 = f32[1,8,8192]{2,1,0:T(8,128)S(1)} fusion(f32[1,8,8192]{2,1,0:T(8,128)S(1)} %broadcast_in_dim.79, s32[]{:T(128)S(6)} %select_n.447, bf16[2048,16,128]{2,1,0:T(8,128)(2,1)} %bitcast.176, bf16[16,8,128]{2,1,0:T(8,128)(2,1)S(1)} %gather_fusion.4, pred[16]{0:T(512)(128)(4,1)S(1)} %get-tuple-element.18), kind=kOutput, calls=%fused_computation.15 | convolution fusion | flops 67125248 | bytes 8487428 | tf_op jit(solution)/shard_map/gabe,cae->gbc/dot_general | solution.py:153
  156.4 0.7 copy-done.1
  157.1 52.7 %reduce-scatter.5.cloned.1.call-done = f32[8,512]{1,0:T(8,128)} async-done(((f32[128,512]{1,0:T(8,128)}), f32[8,512]{1,0:T(8,128)}) %reduce-scatter.5.cloned.1.call-update) | async-done | bytes 16400 | tf_op jit(solution)/shard_map/reduce_scatter | solution.py:159
  209.8 1.3 convert_bitcast_fusion
  (95 shorter events, 5.9 us)
Async XLA Ops:
  6.5 51.0 %copy-start = (bf16[2,1024,512]{2,1,0:T(8,128)(2,1)S(1)}, bf16[2,1024,512]{2,1,0:T(8,128)(2,1)}, u32[]{:S(2)}) copy-start(bf16[2,1024,512]{2,1,0:T(8,128)(2,1)} %param.13) | copy-start | bytes 6291460
  6.5 113.0 %reduce-scatter.3.cloned.1.call-start = ((), (), s32[]{:S(2)}) async-start(), calls=%async_computation.2 | async-start | bytes 417792 | tf_op jit(solution)/shard_map/reduce_scatter | solution.py:90
  6.5 9.4 %collective-permute-start = (bf16[1,8,512]{2,1,0:T(8,128)(2,1)}, bf16[1,8,512]{2,1,0:T(8,128)(2,1)S(1)}, u32[]{:S(2)}, u32[]{:S(2)}) collective-permute-start(bf16[1,8,512]{2,1,0:T(8,128)(2,1)} %param.9), channel_id=1, source_target_pairs={{0,1},{1,2},{2,3},{3,4},{4,5},{5,6},{6,7},{7,8},{8,9},{9,10},{10,1... | collective-permute-start | bytes 24584 | tf_op jit(solution)/shard_map/ppermute | solution.py:52
  7.0 9.1 %collective-permute-start.1 = (bf16[1,8,512]{2,1,0:T(8,128)(2,1)}, bf16[1,8,512]{2,1,0:T(8,128)(2,1)S(1)}, u32[]{:S(2)}, u32[]{:S(2)}) collective-permute-start(bf16[1,8,512]{2,1,0:T(8,128)(2,1)} %param.9), channel_id=1, source_target_pairs={{0,15},{1,0},{2,1},{3,2},{4,3},{5,4},{6,5},{7,6},{8,7},{9,8},{10,9... | collective-permute-start | bytes 24584 | tf_op jit(solution)/shard_map/ppermute | solution.py:55
  16.0 5.9 %collective-permute-start.2 = (bf16[1,8,512]{2,1,0:T(8,128)(2,1)S(1)}, bf16[1,8,512]{2,1,0:T(8,128)(2,1)S(1)}, u32[]{:S(2)}, u32[]{:S(2)}) collective-permute-start(bf16[1,8,512]{2,1,0:T(8,128)(2,1)S(1)} %collective-permute-done), channel_id=1, source_target_pairs={{0,1},{1,2},{2,3},{3,4},{4,5},{5,6},{6,7},{7,8},{8,9},{9,10},{10,1... | collective-permute-start | bytes 24584 | tf_op jit(solution)/shard_map/ppermute | solution.py:52
  16.1 5.8 %collective-permute-start.3 = (bf16[1,8,512]{2,1,0:T(8,128)(2,1)S(1)}, bf16[1,8,512]{2,1,0:T(8,128)(2,1)S(1)}, u32[]{:S(2)}, u32[]{:S(2)}) collective-permute-start(bf16[1,8,512]{2,1,0:T(8,128)(2,1)S(1)} %collective-permute-done.1), channel_id=1, source_target_pairs={{0,15},{1,0},{2,1},{3,2},{4,3},{5,4},{6,5},{7,6},{8,7},{9,8},{10,9... | collective-permute-start | bytes 24584 | tf_op jit(solution)/shard_map/ppermute | solution.py:55
  21.8 5.8 %collective-permute-start.4 = (bf16[1,8,512]{2,1,0:T(8,128)(2,1)S(1)}, bf16[1,8,512]{2,1,0:T(8,128)(2,1)S(1)}, u32[]{:S(2)}, u32[]{:S(2)}) collective-permute-start(bf16[1,8,512]{2,1,0:T(8,128)(2,1)S(1)} %collective-permute-done.2), channel_id=1, source_target_pairs={{0,1},{1,2},{2,3},{3,4},{4,5},{5,6},{6,7},{7,8},{8,9},{9,10},{10,1... | collective-permute-start | bytes 24584 | tf_op jit(solution)/shard_map/ppermute | solution.py:52
  21.9 5.8 %collective-permute-start.5 = (bf16[1,8,512]{2,1,0:T(8,128)(2,1)S(1)}, bf16[1,8,512]{2,1,0:T(8,128)(2,1)S(1)}, u32[]{:S(2)}, u32[]{:S(2)}) collective-permute-start(bf16[1,8,512]{2,1,0:T(8,128)(2,1)S(1)} %collective-permute-done.3), channel_id=1, source_target_pairs={{0,15},{1,0},{2,1},{3,2},{4,3},{5,4},{6,5},{7,6},{8,7},{9,8},{10,9... | collective-permute-start | bytes 24584 | tf_op jit(solution)/shard_map/ppermute | solution.py:55
  27.6 5.8 %collective-permute-start.6 = (bf16[1,8,512]{2,1,0:T(8,128)(2,1)S(1)}, bf16[1,8,512]{2,1,0:T(8,128)(2,1)S(1)}, u32[]{:S(2)}, u32[]{:S(2)}) collective-permute-start(bf16[1,8,512]{2,1,0:T(8,128)(2,1)S(1)} %collective-permute-done.4), channel_id=1, source_target_pairs={{0,1},{1,2},{2,3},{3,4},{4,5},{5,6},{6,7},{7,8},{8,9},{9,10},{10,1... | collective-permute-start | bytes 24584 | tf_op jit(solution)/shard_map/ppermute | solution.py:52
  27.7 5.8 %collective-permute-start.7 = (bf16[1,8,512]{2,1,0:T(8,128)(2,1)S(1)}, bf16[1,8,512]{2,1,0:T(8,128)(2,1)S(1)}, u32[]{:S(2)}, u32[]{:S(2)}) collective-permute-start(bf16[1,8,512]{2,1,0:T(8,128)(2,1)S(1)} %collective-permute-done.5), channel_id=1, source_target_pairs={{0,15},{1,0},{2,1},{3,2},{4,3},{5,4},{6,5},{7,6},{8,7},{9,8},{10,9... | collective-permute-start | bytes 24584 | tf_op jit(solution)/shard_map/ppermute | solution.py:55
  33.4 5.8 %collective-permute-start.8 = (bf16[1,8,512]{2,1,0:T(8,128)(2,1)S(1)}, bf16[1,8,512]{2,1,0:T(8,128)(2,1)S(1)}, u32[]{:S(2)}, u32[]{:S(2)}) collective-permute-start(bf16[1,8,512]{2,1,0:T(8,128)(2,1)S(1)} %collective-permute-done.6), channel_id=1, source_target_pairs={{0,1},{1,2},{2,3},{3,4},{4,5},{5,6},{6,7},{7,8},{8,9},{9,10},{10,1... | collective-permute-start | bytes 24584 | tf_op jit(solution)/shard_map/ppermute | solution.py:52
  33.4 5.8 %collective-permute-start.9 = (bf16[1,8,512]{2,1,0:T(8,128)(2,1)S(1)}, bf16[1,8,512]{2,1,0:T(8,128)(2,1)S(1)}, u32[]{:S(2)}, u32[]{:S(2)}) collective-permute-start(bf16[1,8,512]{2,1,0:T(8,128)(2,1)S(1)} %collective-permute-done.7), channel_id=1, source_target_pairs={{0,15},{1,0},{2,1},{3,2},{4,3},{5,4},{6,5},{7,6},{8,7},{9,8},{10,9... | collective-permute-start | bytes 24584 | tf_op jit(solution)/shard_map/ppermute | solution.py:55
  39.2 5.8 %collective-permute-start.10 = (bf16[1,8,512]{2,1,0:T(8,128)(2,1)S(1)}, bf16[1,8,512]{2,1,0:T(8,128)(2,1)S(1)}, u32[]{:S(2)}, u32[]{:S(2)}) collective-permute-start(bf16[1,8,512]{2,1,0:T(8,128)(2,1)S(1)} %collective-permute-done.8), channel_id=1, source_target_pairs={{0,1},{1,2},{2,3},{3,4},{4,5},{5,6},{6,7},{7,8},{8,9},{9,10},{10,1... | collective-permute-start | bytes 24584 | tf_op jit(solution)/shard_map/ppermute | solution.py:52
  39.2 5.8 %collective-permute-start.11 = (bf16[1,8,512]{2,1,0:T(8,128)(2,1)S(1)}, bf16[1,8,512]{2,1,0:T(8,128)(2,1)S(1)}, u32[]{:S(2)}, u32[]{:S(2)}) collective-permute-start(bf16[1,8,512]{2,1,0:T(8,128)(2,1)S(1)} %collective-permute-done.9), channel_id=1, source_target_pairs={{0,15},{1,0},{2,1},{3,2},{4,3},{5,4},{6,5},{7,6},{8,7},{9,8},{10,9... | collective-permute-start | bytes 24584 | tf_op jit(solution)/shard_map/ppermute | solution.py:55
  44.9 5.8 %collective-permute-start.12 = (bf16[1,8,512]{2,1,0:T(8,128)(2,1)S(1)}, bf16[1,8,512]{2,1,0:T(8,128)(2,1)S(1)}, u32[]{:S(2)}, u32[]{:S(2)}) collective-permute-start(bf16[1,8,512]{2,1,0:T(8,128)(2,1)S(1)} %collective-permute-done.10), channel_id=1, source_target_pairs={{0,1},{1,2},{2,3},{3,4},{4,5},{5,6},{6,7},{7,8},{8,9},{9,10},{10,1... | collective-permute-start | bytes 24584 | tf_op jit(solution)/shard_map/ppermute | solution.py:52
  45.0 5.8 %collective-permute-start.13 = (bf16[1,8,512]{2,1,0:T(8,128)(2,1)S(1)}, bf16[1,8,512]{2,1,0:T(8,128)(2,1)S(1)}, u32[]{:S(2)}, u32[]{:S(2)}) collective-permute-start(bf16[1,8,512]{2,1,0:T(8,128)(2,1)S(1)} %collective-permute-done.11), channel_id=1, source_target_pairs={{0,15},{1,0},{2,1},{3,2},{4,3},{5,4},{6,5},{7,6},{8,7},{9,8},{10,9... | collective-permute-start | bytes 24584 | tf_op jit(solution)/shard_map/ppermute | solution.py:55
  50.7 5.8 %collective-permute-start.14 = (bf16[1,8,512]{2,1,0:T(8,128)(2,1)S(1)}, bf16[1,8,512]{2,1,0:T(8,128)(2,1)S(1)}, u32[]{:S(2)}, u32[]{:S(2)}) collective-permute-start(bf16[1,8,512]{2,1,0:T(8,128)(2,1)S(1)} %collective-permute-done.12), channel_id=1, source_target_pairs={{0,1},{1,2},{2,3},{3,4},{4,5},{5,6},{6,7},{7,8},{8,9},{9,10},{10,1... | collective-permute-start | bytes 24584 | tf_op jit(solution)/shard_map/ppermute | solution.py:52
  58.2 8.0 %copy-start.2 = (s32[1,8]{1,0:T(1,128)S(1)}, s32[1,8]{1,0:T(1,128)}, u32[]{:S(2)}) copy-start(s32[1,8]{1,0:T(1,128)} %param.17) | copy-start | bytes 100
  66.1 143.8 %reduce-scatter.5.cloned.1.call-start = ((), (), s32[]{:S(2)}) async-start(), calls=%async_computation.3 | async-start | bytes 278528 | tf_op jit(solution)/shard_map/reduce_scatter | solution.py:159
  120.3 1.2 collective-permute-start.15
  125.2 4.0 %collective-permute-start.16 = (f32[8,4]{0,1:T(4,128)S(1)}, f32[8,4]{0,1:T(4,128)S(1)}, u32[]{:S(2)}, u32[]{:S(2)}) collective-permute-start(f32[8,4]{0,1:T(4,128)S(1)} %select_bitcast_fusion.2), channel_id=1, source_target_pairs={{0,1},{1,0},{2,3},{3,2},{4,5},{5,4},{6,7},{7,6},{8,9},{9,8},{10,11... | collective-permute-start | bytes 392 | tf_op jit(solution)/shard_map/ppermute | solution.py:19
  125.7 3.5 %collective-permute-start.18 = (f32[8,4]{0,1:T(4,128)S(1)}, f32[8,4]{0,1:T(4,128)S(1)}, u32[]{:S(2)}, u32[]{:S(2)}) collective-permute-start(f32[8,4]{0,1:T(4,128)S(1)} %select_bitcast_fusion.1), channel_id=1, source_target_pairs={{0,1},{1,0},{2,3},{3,2},{4,5},{5,4},{6,7},{7,6},{8,9},{9,8},{10,11... | collective-permute-start | bytes 392 | tf_op jit(solution)/shard_map/ppermute | solution.py:19
  129.0 1.2 collective-permute-start.17
  156.4 0.7 copy-start.1
Sparse Core Ops, SparseCore 0:
  66.2 53.3 reduce-scatter.2
  157.2 52.5 reduce-scatter.4
